TPU v7x, 256 devices: a whole 4x4x8 slice. The times are simulated.
256 devices in a mesh: nodes: 64 (over z, y, core), mp: 4 (over x).
Axes of the slice: x: 4, y: 4, z: 8, core: 2. Of those that a mesh axis runs over, the one named last changes fastest.
Arguments:
- event_feats: bfloat16 [65536, 512], P('nodes'), may hold values from -6 to 6
- event_owner: int32 [65536, 1], P('nodes'), may hold values from 0 to 63; in each aligned block of 1024 rows (0 to 1023, 1024 to 2047, ...) at most 32 rows name the same one
- event_slot: int32 [65536], P('nodes'), may hold values from 0 to 255
- memory: bfloat16 [16384, 1024], P('nodes'), may hold values from -6 to 6
- w_msg_event: bfloat16 [512, 2048], P(None, 'mp'), may hold values from -0.25 to 0.25
- w_msg_state: bfloat16 [1024, 2048], P(None, 'mp'), may hold values from -0.1875 to 0.1875
- b_msg: float32 [2048], P('mp'), may hold values from -3 to 3
- w_msg_out: bfloat16 [2048, 1024], P('mp'), may hold values from -0.125 to 0.125
- b_out: float32 [1024], replicated, may hold values from -3 to 3
- w_input: bfloat16 [3, 1024, 1024], P(None, None, 'mp'), may hold values from -0.1875 to 0.1875
- w_hidden: bfloat16 [3, 1024, 1024], P(None, None, 'mp'), may hold values from -0.1875 to 0.1875
- b_input: float32 [3, 1024], P(None, 'mp'), may hold values from -3 to 3
- b_hidden: float32 [3, 1024], P(None, 'mp'), may hold values from -3 to 3
- state_slots: int32 [4096, 32], P('nodes'), may hold values from 0 to 255
- neighbours: int32 [16384, 10], P('nodes'), may hold values from 0 to 2047
- query_slots: int32 [16384], P('nodes'), may hold values from 0 to 255
- w_neigh: bfloat16 [1024, 1024], P('mp'), may hold values from -0.1875 to 0.1875
- w_self: bfloat16 [1024, 1024], P('mp'), may hold values from -0.1875 to 0.1875
- b_embed: float32 [1024], replicated, may hold values from -3 to 3
Outputs:
- new_memory: bfloat16 [16384, 1024], P('nodes', 'mp')
- embedding: bfloat16 [16384, 1024], P(('nodes', 'mp'))
Inputs may be any that keep to these rules, and one draw needn't show every extreme that they name: `event_owner`: among the 1024 events of one block of events, at most 32 name the same owner, and in every draw some owner is named exactly 32 times by some block.
All inputs are finite; a program needn't handle non-finite values.
Results may differ from a plain program's by a relative error of at most 0.014.
Values may be sent and summed in bfloat16 or wider, within the bound.
No kernel may reach another device: no remote copies, remote signals or barrier semaphores. Data moves between devices by JAX's collectives and lax.ppermute only.
A program may use at most 64 MiB of HBM per device.

v0:
```python
import jax
import jax.numpy as jnp
from jax import lax
from jax.sharding import PartitionSpec as P

F32 = jnp.float32
BF16 = jnp.bfloat16


def one_hot(index, size, dtype=BF16):
    return (index[:, None] == lax.broadcasted_iota(jnp.int32, (1, size), 1)).astype(dtype)


def one_hot_t(index, size, dtype=BF16):
    return (lax.broadcasted_iota(jnp.int32, (size, 1), 0) == index[None, :]).astype(dtype)


def split_dot(x32, w):
    hi = x32.astype(BF16)
    lo = (x32 - hi.astype(F32)).astype(BF16)
    return jnp.dot(hi, w, preferred_element_type=F32) + jnp.dot(lo, w, preferred_element_type=F32)


def per_device(
    event_feats,
    event_owner,
    event_slot,
    memory,
    w_msg_event,
    w_msg_state,
    b_msg,
    w_msg_out,
    b_out,
    w_input,
    w_hidden,
    b_input,
    b_hidden,
    state_slots,
    neighbours,
    query_slots,
    w_neigh,
    w_self,
    b_embed,
):
    owner_count = lax.axis_size("nodes")
    share_count = lax.axis_size("mp")
    mp_index = lax.axis_index("mp")
    event_rows = event_feats.shape[0]
    mem_rows = memory.shape[0]
    mem_width = memory.shape[1]
    col_share = mem_width // share_count
    capacity = 2 * event_rows // owner_count
    send_rows = owner_count * capacity
    owner = event_owner[:, 0]
    match = owner[:, None] == lax.broadcasted_iota(jnp.int32, (1, owner_count), 1)
    earlier = (
        lax.broadcasted_iota(jnp.int32, (event_rows, event_rows), 1)
        < lax.broadcasted_iota(jnp.int32, (event_rows, event_rows), 0)
    ).astype(BF16)
    before = jnp.dot(earlier, match.astype(BF16), preferred_element_type=F32)
    place = jnp.sum(jnp.where(match, before, 0.0), axis=1).astype(jnp.int32)
    target = owner * capacity + place
    route = one_hot_t(target, send_rows)
    feat_buffer = jnp.dot(route, event_feats, preferred_element_type=F32).astype(BF16)
    slot_col = jnp.broadcast_to((event_slot + 1).astype(BF16)[:, None], (event_rows, 128))
    id_buffer = jnp.dot(route, slot_col, preferred_element_type=F32)[:, 0].astype(jnp.int32) - 1
    feat_buffer = feat_buffer.reshape(owner_count, capacity, event_feats.shape[1])
    id_buffer = id_buffer.reshape(owner_count, capacity)
    arrived = lax.all_to_all(feat_buffer, "nodes", split_axis=0, concat_axis=0, tiled=True)
    arrived_ids = lax.all_to_all(id_buffer, "nodes", split_axis=0, concat_axis=0, tiled=True)
    arrived = arrived.reshape(send_rows, event_feats.shape[1])
    arrived_ids = arrived_ids.reshape(send_rows)
    seg = one_hot_t(arrived_ids, mem_rows)
    seg_t = one_hot(arrived_ids, mem_rows)
    counts = jnp.sum(seg.astype(F32), axis=1)
    state_proj = jnp.dot(memory, w_msg_state, preferred_element_type=F32)
    sp_hi = state_proj.astype(BF16)
    sp_lo = (state_proj - sp_hi.astype(F32)).astype(BF16)
    gathered = jnp.dot(seg_t, sp_hi, preferred_element_type=F32) + jnp.dot(
        seg_t, sp_lo, preferred_element_type=F32
    )
    pre = jnp.dot(arrived, w_msg_event, preferred_element_type=F32) + gathered + b_msg
    hidden_msg = jax.nn.relu(pre).astype(BF16)
    hidden_sum = jnp.dot(seg, hidden_msg, preferred_element_type=F32)
    partial_total = split_dot(hidden_sum, w_msg_out)
    divisor = jnp.maximum(counts, 1.0)[:, None]
    msg_total = lax.psum(partial_total.astype(BF16), "mp").astype(F32)
    aggregate = (msg_total / divisor + b_out).astype(BF16)
    gates_in = (
        jnp.einsum("nd,gdc->gnc", aggregate, w_input, preferred_element_type=F32)
        + b_input[:, None, :]
    )
    gates_st = (
        jnp.einsum("nd,gdc->gnc", memory, w_hidden, preferred_element_type=F32)
        + b_hidden[:, None, :]
    )
    reset_gate = jax.nn.sigmoid(gates_in[0] + gates_st[0])
    update_gate = jax.nn.sigmoid(gates_in[1] + gates_st[1])
    candidate = jnp.tanh(gates_in[2] + reset_gate * gates_st[2])
    old_state = lax.dynamic_slice_in_dim(memory, mp_index * col_share, col_share, 1).astype(F32)
    updated = (1.0 - update_gate) * candidate + update_gate * old_state
    new_memory = jnp.where((counts > 0.0)[:, None], updated, old_state).astype(BF16)
    pick = one_hot(state_slots.reshape(-1), mem_rows)
    outgoing = jnp.dot(pick, new_memory, preferred_element_type=F32).astype(BF16)
    outgoing = outgoing.reshape(state_slots.shape[0], state_slots.shape[1], col_share)
    relayed = lax.all_to_all(outgoing, "nodes", split_axis=0, concat_axis=0, tiled=True)
    relayed = relayed.reshape(relayed.shape[0] * relayed.shape[1], col_share)
    recv_rows = relayed.shape[0]
    neigh_count = one_hot(neighbours[:, 0], recv_rows, F32)
    for k in range(1, neighbours.shape[1]):
        neigh_count = neigh_count + one_hot(neighbours[:, k], recv_rows, F32)
    neigh_total = jnp.dot(neigh_count.astype(BF16), relayed, preferred_element_type=F32)
    neigh_mean = (neigh_total / neighbours.shape[1]).astype(BF16)
    self_state = jnp.dot(
        one_hot(query_slots, mem_rows), new_memory, preferred_element_type=F32
    ).astype(BF16)
    summed = lax.psum_scatter(
        (
            jnp.dot(neigh_mean, w_neigh, preferred_element_type=F32)
            + jnp.dot(self_state, w_self, preferred_element_type=F32)
        ).astype(BF16),
        "mp",
        scatter_dimension=0,
        tiled=True,
    ).astype(F32)
    embedding = jax.nn.relu(summed + b_embed).astype(BF16)
    return (new_memory, embedding)


def solution(mesh):
    in_specs = (
        P("nodes", None),
        P("nodes", None),
        P("nodes"),
        P("nodes", None),
        P(None, "mp"),
        P(None, "mp"),
        P("mp"),
        P("mp", None),
        P(),
        P(None, None, "mp"),
        P(None, None, "mp"),
        P(None, "mp"),
        P(None, "mp"),
        P("nodes", None),
        P("nodes", None),
        P("nodes"),
        P("mp", None),
        P("mp", None),
        P(),
    )
    out_specs = (P("nodes", "mp"), P(("nodes", "mp"), None))
    return jax.shard_map(
        per_device, mesh=mesh, in_specs=in_specs, out_specs=out_specs, check_vma=False
    )
```

profile of v0, /device:TPU:8, one launch (start us, length us, event | category | flops | bytes accessed | tf_op | source)
XLA Modules:
  0.0 229.8 jit_solution(13765049817450807412)
XLA Ops:
  7.2 0.0 copy-start
  7.2 0.8 add_convert_fusion.4
  8.0 0.2 reshape.97
  8.2 1.4 fusion.17
  9.6 0.0 copy-start.12
  9.6 0.8 convert_add_fusion
  10.4 1.6 fusion.19
  11.9 0.7 sub.16
  12.6 12.1 %all-to-all-start = ((s32[64,1,32]{2,1,0:T(1,128)}), s32[64,1,32]{2,1,0:T(1,128)S(1)}, u32[]{:S(2)}, u32[]{:S(2)}) async-start(s32[64,1,32]{2,1,0:T(1,128)} %bitcast.1), calls=%async_computation | async-start | bytes 65536 | tf_op jit(solution)/shard_map/all_to_all | solution.py:70
  24.7 0.0 copy-done.12
  24.7 3.7 %fusion.5 = bf16[2048,512]{1,0:T(8,128)(2,1)} fusion(bf16[1024,512]{1,0:T(8,128)(2,1)S(1)} %copy-done.12, s32[1024]{0:T(1024)S(1)} %convert_add_fusion), kind=kOutput, calls=%fused_computation.8 | convolution fusion | flops 2150629376 | bytes 3149824 | tf_op jit(solution)/shard_map/dot_general | solution.py:64
  28.4 4.9 %all-to-all-done = s32[64,1,32]{2,1,0:T(1,128)S(1)} async-done(((s32[64,1,32]{2,1,0:T(1,128)}), s32[64,1,32]{2,1,0:T(1,128)S(1)}, u32[]{:S(2)}, u32[]{:S(2)}) %all-to-all-start) | async-done | bytes 8224 | tf_op jit(solution)/shard_map/all_to_all | solution.py:70
  33.3 6.5 %all-to-all-start.1 = ((bf16[64,32,512]{2,1,0:T(8,128)(2,1)}), bf16[64,32,512]{2,1,0:T(8,128)(2,1)}, u32[]{:S(2)}, u32[]{:S(2)}) async-start(bf16[64,32,512]{2,1,0:T(8,128)(2,1)} %bitcast.51), calls=%async_computation.1 | async-start | bytes 4194304 | tf_op jit(solution)/shard_map/all_to_all | solution.py:69
  39.8 0.0 copy-start.13
  39.8 0.2 all-reduce.2.cloned.1.call-start
  40.1 0.1 copy.33
  40.2 0.1 eq.285
  40.2 0.0 copy-done.3
  40.2 1.5 fusion.78
  41.7 2.5 %fusion.13 = f32[3,256,256]{2,1,0:T(8,128)} fusion(bf16[3,1024,256]{2,1,0:T(8,128)(2,1)S(1)} %copy-done, bf16[256,1024]{1,0:T(8,128)(2,1)} %param.22, f32[3,256]{1,0:T(4,128)S(1)} %copy-done.13), kind=kOutput, calls=%fused_computation.35 | convolution fusion | flops 402849792 | bytes 2886656 | tf_op jit(solution)/shard_map/nd,gdc->gnc/dot_general | solution.py:94
  44.3 0.5 broadcast.59
  44.8 0.7 reduce.7
  45.5 0.1 eq.239
  45.6 2.4 %fusion.8 = f32[2048,512]{1,0:T(8,128)} fusion(s32[2048]{0:T(1024)S(1)} %eq.239, f32[256,512]{1,0:T(8,128)S(1)} %fusion.78), kind=kOutput, calls=%fused_computation.25 | convolution fusion | flops 537526272 | bytes 4726784 | tf_op jit(solution)/shard_map/dot_general | solution.py:79
  48.0 43.1 %all-to-all-done.1 = bf16[64,32,512]{2,1,0:T(8,128)(2,1)} async-done(((bf16[64,32,512]{2,1,0:T(8,128)(2,1)}), bf16[64,32,512]{2,1,0:T(8,128)(2,1)}, u32[]{:S(2)}, u32[]{:S(2)}) %all-to-all-start.1) | async-done | bytes 2097184 | tf_op jit(solution)/shard_map/all_to_all | solution.py:69
  91.1 4.8 %fusion.77 = f32[2048,512]{1,0:T(8,128)} fusion(bf16[2048,512]{1,0:T(8,128)(2,1)} %bitcast.3, bf16[512,512]{1,0:T(8,128)(2,1)S(1)} %copy-done.5), kind=kOutput, calls=%fused_computation.104 | convolution fusion | flops 1073741824 | bytes 6815744 | tf_op jit(solution)/shard_map/dot_general | solution.py:82
  95.9 6.0 %fusion.9 = f32[256,512]{1,0:T(8,128)} fusion(s32[2048]{0:T(1024)S(1)} %eq.239, f32[2048,512]{1,0:T(8,128)} %fusion.77, f32[2048,512]{1,0:T(8,128)} %fusion.8, f32[512]{0:T(512)S(1)} %copy-done.16, f32[256,512]{1,0:T(8,128)S(1)} %fusion.78), kind=kOutput, calls=%fused_computation.28 | convolution fusion | flops 1080557568 | bytes 9447424 | tf_op jit(solution)/shard_map/dot_general | solution.py:84
  101.9 1.5 fusion.68
  103.5 0.0 copy-start.14
  103.5 0.0 copy-start.15
  103.5 1.2 fusion.11
  104.7 0.0 all-reduce.2.cloned.1.call-update
  104.8 0.3 convert_reduce_fusion
  105.1 44.3 %all-reduce.2.cloned.1.call-done = bf16[256,1024]{1,0:T(8,128)(2,1)} async-done(((bf16[256,1024]{1,0:T(8,128)(2,1)}), bf16[256,1024]{1,0:T(8,128)(2,1)}) %all-reduce.2.cloned.1.call-update) | async-done | bytes 524304 | tf_op jit(solution)/shard_map/psum | solution.py:87
  149.4 2.2 fusion.14
  151.6 1.1 fusion.50
  152.7 0.0 copy-start.6
  152.7 0.0 copy-start.9
  152.8 1.5 convolution_convert_fusion
  154.3 10.6 %all-to-all-start.2 = ((bf16[64,32,256]{2,1,0:T(8,128)(2,1)}), bf16[64,32,256]{2,1,0:T(8,128)(2,1)S(1)}, u32[]{:S(2)}, u32[]{:S(2)}) async-start(bf16[64,32,256]{2,1,0:T(8,128)(2,1)} %bitcast.53), calls=%async_computation.2 | async-start | bytes 2097152 | tf_op jit(solution)/shard_map/all_to_all | solution.py:106
  164.9 0.0 reduce-scatter.2.cloned.1.call-start
  164.9 28.7 %all-to-all-done.2 = bf16[64,32,256]{2,1,0:T(8,128)(2,1)S(1)} async-done(((bf16[64,32,256]{2,1,0:T(8,128)(2,1)}), bf16[64,32,256]{2,1,0:T(8,128)(2,1)S(1)}, u32[]{:S(2)}, u32[]{:S(2)}) %all-to-all-start.2) | async-done | bytes 1048608 | tf_op jit(solution)/shard_map/all_to_all | solution.py:106
  193.6 5.2 %fusion.18 = f32[256,1024]{1,0:T(8,128)} fusion(bf16[256,1024]{1,0:T(8,128)(2,1)} %param.35, bf16[2048,256]{1,0:T(8,128)(2,1)S(1)} %bitcast.52, s32[256]{0:T(256)S(1)} %bitcast.64, s32[256]{0:T(256)S(1)} %bitcast.65, s32[256]{0:T(256)S(1)} %bitcast.57, s32[256]{0:T(256)S(1)} %bitcast.58, s32[256]{0:T(256)S(1)} %bitcast.59, s32[256]{0:T(256)S(1)} %bitcast.60, ...), kind=kOutput, calls=%fused_computation.43 | convolution fusion | flops 418512896 | bytes 2631680 | tf_op jit(solution)/shard_map/dot_general | solution.py:119
  198.8 0.0 copy-start.10
  198.9 2.5 %fusion.12 = bf16[256,1024]{1,0:T(8,128)(2,1)} fusion(f32[256,1024]{1,0:T(8,128)} %fusion.18, bf16[256,1024]{1,0:T(8,128)(2,1)S(1)} %copy-done.7, bf16[256,256]{1,0:T(8,128)(2,1)S(1)} %fusion.50, s32[256]{0:T(256)S(1)} %copy-done.11), kind=kOutput, calls=%fused_computation.33 | convolution fusion | flops 168427520 | bytes 2229248 | tf_op jit(solution)/shard_map/dot_general | solution.py:120
  201.4 0.0 reduce-scatter.2.cloned.1.call-update
  201.4 20.0 %reduce-scatter.2.cloned.1.call-done = bf16[64,1024]{1,0:T(8,128)(2,1)} async-done(((bf16[256,1024]{1,0:T(8,128)(2,1)}), bf16[64,1024]{1,0:T(8,128)(2,1)}) %reduce-scatter.2.cloned.1.call-update) | async-done | bytes 131088 | tf_op jit(solution)/shard_map/reduce_scatter | solution.py:117
  221.4 1.6 maximum_convert_fusion.1
  (27 shorter events, 0.1 us)
Async XLA Ops:
  7.2 34.6 %copy-start = (bf16[3,1024,256]{2,1,0:T(8,128)(2,1)S(1)}, bf16[3,1024,256]{2,1,0:T(8,128)(2,1)}, u32[]{:S(2)}) copy-start(bf16[3,1024,256]{2,1,0:T(8,128)(2,1)} %param.29) | copy-start | bytes 4718596
  9.6 15.2 %copy-start.12 = (bf16[1024,512]{1,0:T(8,128)(2,1)S(1)}, bf16[1024,512]{1,0:T(8,128)(2,1)}, u32[]{:S(2)}) copy-start(bf16[1024,512]{1,0:T(8,128)(2,1)} %param.19) | copy-start | bytes 3145732
  12.6 20.7 %all-to-all-start = ((s32[64,1,32]{2,1,0:T(1,128)}), s32[64,1,32]{2,1,0:T(1,128)S(1)}, u32[]{:S(2)}, u32[]{:S(2)}) async-start(s32[64,1,32]{2,1,0:T(1,128)} %bitcast.1), calls=%async_computation | async-start | bytes 65536 | tf_op jit(solution)/shard_map/all_to_all | solution.py:70
  33.3 6.8 %copy-start.8 = (s32[64,32]{0,1:T(8,128)S(1)}, s32[64,32]{0,1:T(8,128)}, u32[]{:S(2)}) copy-start(s32[64,32]{0,1:T(8,128)} %param.32) | copy-start | bytes 24580
  33.3 6.9 %copy-start.3 = (bf16[1024,512]{1,0:T(8,128)(2,1)S(1)}, bf16[1024,512]{1,0:T(8,128)(2,1)}, u32[]{:S(2)}) copy-start(bf16[1024,512]{1,0:T(8,128)(2,1)} %param.24) | copy-start | bytes 3145732
  33.3 57.8 %all-to-all-start.1 = ((bf16[64,32,512]{2,1,0:T(8,128)(2,1)}), bf16[64,32,512]{2,1,0:T(8,128)(2,1)}, u32[]{:S(2)}, u32[]{:S(2)}) async-start(bf16[64,32,512]{2,1,0:T(8,128)(2,1)} %bitcast.51), calls=%async_computation.1 | async-start | bytes 4194304 | tf_op jit(solution)/shard_map/all_to_all | solution.py:69
  39.8 1.9 copy-start.13
  39.8 109.6 %all-reduce.2.cloned.1.call-start = ((), (), s32[]{:S(2)}) async-start(), calls=%async_computation.4 | async-start | bytes 1048576 | tf_op jit(solution)/shard_map/psum | solution.py:87
  45.6 45.5 %copy-start.5 = (bf16[512,512]{1,0:T(8,128)(2,1)S(1)}, bf16[512,512]{1,0:T(8,128)(2,1)}, u32[]{:S(2)}) copy-start(bf16[512,512]{1,0:T(8,128)(2,1)} %param.23) | copy-start | bytes 1572868
  91.1 4.8 %copy-start.16 = (f32[512]{0:T(512)S(1)}, f32[512]{0:T(512)}, u32[]{:S(2)}) copy-start(f32[512]{0:T(512)} %param.25) | copy-start | bytes 6148
  95.9 6.0 %copy-start.1 = (bf16[512,1024]{1,0:T(8,128)(2,1)S(1)}, bf16[512,1024]{1,0:T(8,128)(2,1)}, u32[]{:S(2)}) copy-start(bf16[512,1024]{1,0:T(8,128)(2,1)} %param.26) | copy-start | bytes 3145732
  101.9 1.6 copy-start.2
  103.5 45.9 %copy-start.14 = (f32[1024]{0:T(1024)S(1)}, f32[1024]{0:T(1024)}, u32[]{:S(2)}) copy-start(f32[1024]{0:T(1024)} %param.27) | copy-start | bytes 12292
  103.5 45.9 %copy-start.15 = (f32[3,256]{1,0:T(4,128)S(1)}, f32[3,256]{1,0:T(4,128)}, u32[]{:S(2)}) copy-start(f32[3,256]{1,0:T(4,128)} %param.30) | copy-start | bytes 9220
  105.1 46.5 %copy-start.4 = (f32[3,256,256]{2,1,0:T(8,128)S(1)}, f32[3,256,256]{2,1,0:T(8,128)}, u32[]{:S(2)}) copy-start(f32[3,256,256]{2,1,0:T(8,128)} %fusion.13) | copy-start | bytes 2359300
  152.7 46.1 %copy-start.6 = (bf16[256,256]{1,0:T(8,128)(2,1)}, bf16[256,256]{1,0:T(8,128)(2,1)S(1)}, u32[]{:S(2)}) copy-start(bf16[256,256]{1,0:T(8,128)(2,1)S(1)} %fusion.50) | copy-start | bytes 393220
  152.7 12.2 %copy-start.9 = (s32[256,10]{0,1:T(8,128)S(1)}, s32[256,10]{0,1:T(8,128)}, u32[]{:S(2)}) copy-start(s32[256,10]{0,1:T(8,128)} %param.33) | copy-start | bytes 30724
  154.3 39.3 %all-to-all-start.2 = ((bf16[64,32,256]{2,1,0:T(8,128)(2,1)}), bf16[64,32,256]{2,1,0:T(8,128)(2,1)S(1)}, u32[]{:S(2)}, u32[]{:S(2)}) async-start(bf16[64,32,256]{2,1,0:T(8,128)(2,1)} %bitcast.53), calls=%async_computation.2 | async-start | bytes 2097152 | tf_op jit(solution)/shard_map/all_to_all | solution.py:106
  164.9 56.5 %reduce-scatter.2.cloned.1.call-start = ((), (), s32[]{:S(2)}) async-start(), calls=%async_computation.5 | async-start | bytes 655360 | tf_op jit(solution)/shard_map/reduce_scatter | solution.py:117
  193.6 5.2 %copy-start.7 = (bf16[256,1024]{1,0:T(8,128)(2,1)S(1)}, bf16[256,1024]{1,0:T(8,128)(2,1)}, u32[]{:S(2)}) copy-start(bf16[256,1024]{1,0:T(8,128)(2,1)} %param.36) | copy-start | bytes 1572868
  193.6 5.2 %copy-start.11 = (s32[256]{0:T(256)S(1)}, s32[256]{0:T(256)}, u32[]{:S(2)}) copy-start(s32[256]{0:T(256)} %param.34) | copy-start | bytes 3076
  198.8 22.5 %copy-start.10 = (f32[1024]{0:T(1024)S(1)}, f32[1024]{0:T(1024)}, u32[]{:S(2)}) copy-start(f32[1024]{0:T(1024)} %param.37) | copy-start | bytes 12292
Sparse Core Ops, SparseCore 0:
  104.9 44.4 all-reduce.1
  201.5 19.8 reduce-scatter.1
where the time goes:
time: 230 us
  waiting for transfers between devices  141 us (61%)
  matrix products  38.1 us (17%)
  starting transfers between devices  29.4 us (13%)
  between operations  14.3 us (6%)
  other arithmetic  5.33 us (2%)
    psum x1, waiting for transfers between devices, per_device(): msg_total = lax.psum(partial_total.astype(BF16), 'mp').astype(F32)  44.3 us
    all_to_all x1, waiting for transfers between devices, per_device(): lax.all_to_all(feat_buffer, 'nodes', split_axis=0, concat_axis=0, tiled=T...  43.1 us
    all_to_all x1, waiting for transfers between devices, per_device(): lax.all_to_all(outgoing, 'nodes', split_axis=0, concat_axis=0, tiled=True)  28.7 us
    reduce_scatter x1, waiting for transfers between devices, per_device(): lax.psum_scatter((jnp.dot(neigh_mean, w_neigh, preferred_element_type=F32...  20 us
    all_to_all x1, starting transfers between devices, per_device(): lax.all_to_all(id_buffer, 'nodes', split_axis=0, concat_axis=0, tiled=True)  12.1 us
    all_to_all x1, starting transfers between devices, per_device(): lax.all_to_all(outgoing, 'nodes', split_axis=0, concat_axis=0, tiled=True)  10.6 us
    all_to_all x1, starting transfers between devices, per_device(): lax.all_to_all(feat_buffer, 'nodes', split_axis=0, concat_axis=0, tiled=T...  6.52 us
    dot_general x1, matrix products, per_device(): hidden_sum = jnp.dot(seg, hidden_msg, preferred_element_type=F32)  5.99 us
  transfers between devices with their start and end apart: 5, of which 5 were waited for; matrix products, arithmetic and copies ran while one was open for 5% of the time, Pallas kernels for 0%

commit v1 on v0

--- a/solution.py
+++ b/solution.py
@@ -84,7 +84,7 @@
     hidden_sum = jnp.dot(seg, hidden_msg, preferred_element_type=F32)
     partial_total = split_dot(hidden_sum, w_msg_out)
     divisor = jnp.maximum(counts, 1.0)[:, None]
-    msg_total = lax.psum(partial_total.astype(BF16), "mp").astype(F32)
+    msg_total = jnp.sum(lax.all_gather(partial_total.astype(BF16), "mp"), axis=0).astype(F32)
     aggregate = (msg_total / divisor + b_out).astype(BF16)
     gates_in = (
         jnp.einsum("nd,gdc->gnc", aggregate, w_input, preferred_element_type=F32)

time: 230 us -> 217 us (0.943)
  waiting for transfers between devices: 141 us -> 127 us
    psum x1 -> x0, waiting for transfers between devices: 44.3 us -> none  [per_device(): msg_total = lax.psum(partial_total.astype(BF16), 'mp').astype(F32)]
    all_gather x0 -> x1, waiting for transfers between devices: none -> 28.6 us  [per_device(): lax.all_gather(partial_total.astype(BF16), 'mp')]
    reduce_sum x0 -> x1, other arithmetic: none -> 2.94 us  [per_device(): jnp.sum(lax.all_gather(partial_total.astype(BF16), 'mp'), axis=0)]
    all_to_all x1, waiting for transfers between devices: 43.1 us -> 45.8 us  [per_device(): lax.all_to_all(feat_buffer, 'nodes', split_axis=0, concat_axis=0, tiled=T...]
where the time goes in v1:
time: 217 us; the launch traced here: 216 us
  waiting for transfers between devices  127 us (59%)
  matrix products  36.1 us (17%)
  starting transfers between devices  29.4 us (14%)
  between operations  14.3 us (7%)
  other arithmetic  7.36 us (3%)
    all_to_all x1, waiting for transfers between devices, per_device(): lax.all_to_all(feat_buffer, 'nodes', split_axis=0, concat_axis=0, tiled=T...  45.8 us
    all_to_all x1, waiting for transfers between devices, per_device(): lax.all_to_all(outgoing, 'nodes', split_axis=0, concat_axis=0, tiled=True)  28.7 us
    all_gather x1, waiting for transfers between devices, per_device(): lax.all_gather(partial_total.astype(BF16), 'mp')  28.6 us
    reduce_scatter x1, waiting for transfers between devices, per_device(): lax.psum_scatter((jnp.dot(neigh_mean, w_neigh, preferred_element_type=F32...  19.5 us
    all_to_all x1, starting transfers between devices, per_device(): lax.all_to_all(id_buffer, 'nodes', split_axis=0, concat_axis=0, tiled=True)  12.1 us
    all_to_all x1, starting transfers between devices, per_device(): lax.all_to_all(outgoing, 'nodes', split_axis=0, concat_axis=0, tiled=True)  10.5 us
    all_to_all x1, starting transfers between devices, per_device(): lax.all_to_all(feat_buffer, 'nodes', split_axis=0, concat_axis=0, tiled=T...  6.52 us
    dot_general x1, matrix products, per_device(): hidden_sum = jnp.dot(seg, hidden_msg, preferred_element_type=F32)  5.99 us
  transfers between devices with their start and end apart: 5, of which 5 were waited for; matrix products, arithmetic and copies ran while one was open for 5% of the time, Pallas kernels for 0%

profile of v1, /device:TPU:8, one launch (start us, length us, event | category | flops | bytes accessed | tf_op | source)
XLA Modules:
  0.0 216.4 jit_solution(16276058005356533700)
XLA Ops:
  7.2 0.0 copy-start
  7.2 0.8 add_convert_fusion.4
  8.0 0.2 reshape.98
  8.2 1.4 fusion.17
  9.6 0.0 copy-start.12
  9.6 0.8 convert_add_fusion
  10.4 1.6 fusion.19
  11.9 0.7 sub.16
  12.6 12.1 %all-to-all-start = ((s32[64,1,32]{2,1,0:T(1,128)}), s32[64,1,32]{2,1,0:T(1,128)S(1)}, u32[]{:S(2)}, u32[]{:S(2)}) async-start(s32[64,1,32]{2,1,0:T(1,128)} %bitcast.1), calls=%async_computation | async-start | bytes 65536 | tf_op jit(solution)/shard_map/all_to_all | solution.py:70
  24.7 3.7 %fusion.5 = bf16[2048,512]{1,0:T(8,128)(2,1)} fusion(bf16[1024,512]{1,0:T(8,128)(2,1)S(1)} %copy-done.12, s32[1024]{0:T(1024)S(1)} %convert_add_fusion), kind=kOutput, calls=%fused_computation.8 | convolution fusion | flops 2150629376 | bytes 3149824 | tf_op jit(solution)/shard_map/dot_general | solution.py:64
  28.4 4.9 %all-to-all-done = s32[64,1,32]{2,1,0:T(1,128)S(1)} async-done(((s32[64,1,32]{2,1,0:T(1,128)}), s32[64,1,32]{2,1,0:T(1,128)S(1)}, u32[]{:S(2)}, u32[]{:S(2)}) %all-to-all-start) | async-done | bytes 8224 | tf_op jit(solution)/shard_map/all_to_all | solution.py:70
  33.3 6.5 %all-to-all-start.1 = ((bf16[64,32,512]{2,1,0:T(8,128)(2,1)}), bf16[64,32,512]{2,1,0:T(8,128)(2,1)}, u32[]{:S(2)}, u32[]{:S(2)}) async-start(bf16[64,32,512]{2,1,0:T(8,128)(2,1)} %bitcast.53), calls=%async_computation.1 | async-start | bytes 4194304 | tf_op jit(solution)/shard_map/all_to_all | solution.py:69
  39.8 0.2 all-gather.3.cloned.1.call-start
  40.1 1.5 fusion.78
  41.5 0.5 broadcast.59
  42.1 0.7 reduce.8
  42.8 0.1 eq.239
  42.9 2.4 %fusion.8 = f32[2048,512]{1,0:T(8,128)} fusion(s32[2048]{0:T(1024)S(1)} %eq.239, f32[256,512]{1,0:T(8,128)S(1)} %fusion.78), kind=kOutput, calls=%fused_computation.25 | convolution fusion | flops 537526272 | bytes 4726784 | tf_op jit(solution)/shard_map/dot_general | solution.py:79
  45.3 45.8 %all-to-all-done.1 = bf16[64,32,512]{2,1,0:T(8,128)(2,1)} async-done(((bf16[64,32,512]{2,1,0:T(8,128)(2,1)}), bf16[64,32,512]{2,1,0:T(8,128)(2,1)}, u32[]{:S(2)}, u32[]{:S(2)}) %all-to-all-start.1) | async-done | bytes 2097184 | tf_op jit(solution)/shard_map/all_to_all | solution.py:69
  91.1 4.8 %fusion.77 = f32[2048,512]{1,0:T(8,128)} fusion(bf16[2048,512]{1,0:T(8,128)(2,1)} %bitcast.3, bf16[512,512]{1,0:T(8,128)(2,1)S(1)} %copy-done.5), kind=kOutput, calls=%fused_computation.104 | convolution fusion | flops 1073741824 | bytes 6815744 | tf_op jit(solution)/shard_map/dot_general | solution.py:82
  95.9 6.0 %fusion.9 = f32[256,512]{1,0:T(8,128)} fusion(s32[2048]{0:T(1024)S(1)} %eq.239, f32[2048,512]{1,0:T(8,128)} %fusion.77, f32[2048,512]{1,0:T(8,128)} %fusion.8, f32[512]{0:T(512)S(1)} %copy-done.16, f32[256,512]{1,0:T(8,128)S(1)} %fusion.78), kind=kOutput, calls=%fused_computation.28 | convolution fusion | flops 1080557568 | bytes 9447424 | tf_op jit(solution)/shard_map/dot_general | solution.py:84
  101.9 1.5 fusion.68
  103.5 0.0 copy-start.8
  103.5 0.0 copy-start.4
  103.5 0.0 copy-start.13
  103.5 1.3 fusion.11
  104.8 0.0 all-gather.3.cloned.1.call-update
  104.8 0.1 copy.33
  104.9 0.1 eq.285
  105.0 0.0 copy-start.14
  105.0 0.0 copy-start.15
  105.0 0.6 fusion.13
  105.6 0.3 convert_reduce_fusion
  105.9 28.6 %all-gather.3.cloned.1.call-done = bf16[1024,1024]{1,0:T(8,128)(2,1)} async-done(((bf16[256,1024]{1,0:T(8,128)(2,1)}), bf16[1024,1024]{1,0:T(8,128)(2,1)}) %all-gather.3.cloned.1.call-update) | async-done | bytes 2097168 | tf_op jit(solution)/shard_map/all_gather | solution.py:87
  134.4 2.9 %reduce_sum.32 = bf16[256,1024]{1,0:T(8,128)(2,1)} reduce(bf16[4,256,1024]{2,1,0:T(8,128)(2,1)} %bitcast.52, bf16[]{:T(256)} %constant.7.clone.1), dimensions={0}, to_apply=%region_2.3 | reduce | flops 786432 | bytes 2621442 | tf_op jit(solution)/shard_map/reduce_sum | solution.py:87
  137.4 2.2 %fusion.14 = f32[3,256,256]{2,1,0:T(8,128)S(1)} fusion(bf16[3,1024,256]{2,1,0:T(8,128)(2,1)} %param.28, bf16[256,1024]{1,0:T(8,128)(2,1)} %reduce_sum.32, f32[1024]{0:T(1024)S(1)} %copy-done.14, f32[256]{0:T(256)S(1)} %broadcast_maximum_fusion, f32[3,256]{1,0:T(4,128)S(1)} %copy-done.15), kind=kOutput, calls=%fused_computation.37 | convolution fusion | flops 403898368 | bytes 2891776 | tf_op jit(solution)/shard_map/nd,gdc->gnc/dot_general | solution.py:90
  139.6 0.2 fusion.50
  139.8 0.0 copy-start.6
  139.8 1.5 convolution_convert_fusion
  141.4 10.5 %all-to-all-start.2 = ((bf16[64,32,256]{2,1,0:T(8,128)(2,1)}), bf16[64,32,256]{2,1,0:T(8,128)(2,1)S(1)}, u32[]{:S(2)}, u32[]{:S(2)}) async-start(bf16[64,32,256]{2,1,0:T(8,128)(2,1)} %bitcast.55), calls=%async_computation.2 | async-start | bytes 2097152 | tf_op jit(solution)/shard_map/all_to_all | solution.py:106
  151.9 0.0 reduce-scatter.2.cloned.1.call-start
  152.0 28.7 %all-to-all-done.2 = bf16[64,32,256]{2,1,0:T(8,128)(2,1)S(1)} async-done(((bf16[64,32,256]{2,1,0:T(8,128)(2,1)}), bf16[64,32,256]{2,1,0:T(8,128)(2,1)S(1)}, u32[]{:S(2)}, u32[]{:S(2)}) %all-to-all-start.2) | async-done | bytes 1048608 | tf_op jit(solution)/shard_map/all_to_all | solution.py:106
  180.7 5.2 %fusion.18 = f32[256,1024]{1,0:T(8,128)} fusion(bf16[256,1024]{1,0:T(8,128)(2,1)} %param.35, bf16[2048,256]{1,0:T(8,128)(2,1)S(1)} %bitcast.54, s32[256]{0:T(256)S(1)} %bitcast.66, s32[256]{0:T(256)S(1)} %bitcast.67, s32[256]{0:T(256)S(1)} %bitcast.59, s32[256]{0:T(256)S(1)} %bitcast.60, s32[256]{0:T(256)S(1)} %bitcast.61, s32[256]{0:T(256)S(1)} %bitcast.62, ...), kind=kOutput, calls=%fused_computation.43 | convolution fusion | flops 418512896 | bytes 2631680 | tf_op jit(solution)/shard_map/dot_general | solution.py:119
  185.9 0.0 copy-start.10
  185.9 2.5 %fusion.12 = bf16[256,1024]{1,0:T(8,128)(2,1)} fusion(f32[256,1024]{1,0:T(8,128)} %fusion.18, bf16[256,1024]{1,0:T(8,128)(2,1)S(1)} %copy-done.7, bf16[256,256]{1,0:T(8,128)(2,1)S(1)} %fusion.50, s32[256]{0:T(256)S(1)} %copy-done.11), kind=kOutput, calls=%fused_computation.33 | convolution fusion | flops 168427520 | bytes 2229248 | tf_op jit(solution)/shard_map/dot_general | solution.py:120
  188.4 0.0 reduce-scatter.2.cloned.1.call-update
  188.5 19.5 %reduce-scatter.2.cloned.1.call-done = bf16[64,1024]{1,0:T(8,128)(2,1)} async-done(((bf16[256,1024]{1,0:T(8,128)(2,1)}), bf16[64,1024]{1,0:T(8,128)(2,1)}) %reduce-scatter.2.cloned.1.call-update) | async-done | bytes 131088 | tf_op jit(solution)/shard_map/reduce_scatter | solution.py:117
  207.9 1.6 maximum_convert_fusion.1
  (28 shorter events, 0.1 us)
Async XLA Ops:
  7.2 97.8 %copy-start = (bf16[3,1024,256]{2,1,0:T(8,128)(2,1)S(1)}, bf16[3,1024,256]{2,1,0:T(8,128)(2,1)}, u32[]{:S(2)}) copy-start(bf16[3,1024,256]{2,1,0:T(8,128)(2,1)} %param.29) | copy-start | bytes 4718596
  9.6 15.2 %copy-start.12 = (bf16[1024,512]{1,0:T(8,128)(2,1)S(1)}, bf16[1024,512]{1,0:T(8,128)(2,1)}, u32[]{:S(2)}) copy-start(bf16[1024,512]{1,0:T(8,128)(2,1)} %param.19) | copy-start | bytes 3145732
  12.6 20.7 %all-to-all-start = ((s32[64,1,32]{2,1,0:T(1,128)}), s32[64,1,32]{2,1,0:T(1,128)S(1)}, u32[]{:S(2)}, u32[]{:S(2)}) async-start(s32[64,1,32]{2,1,0:T(1,128)} %bitcast.1), calls=%async_computation | async-start | bytes 65536 | tf_op jit(solution)/shard_map/all_to_all | solution.py:70
  33.3 6.8 %copy-start.3 = (bf16[1024,512]{1,0:T(8,128)(2,1)S(1)}, bf16[1024,512]{1,0:T(8,128)(2,1)}, u32[]{:S(2)}) copy-start(bf16[1024,512]{1,0:T(8,128)(2,1)} %param.24) | copy-start | bytes 3145732
  33.3 57.8 %all-to-all-start.1 = ((bf16[64,32,512]{2,1,0:T(8,128)(2,1)}), bf16[64,32,512]{2,1,0:T(8,128)(2,1)}, u32[]{:S(2)}, u32[]{:S(2)}) async-start(bf16[64,32,512]{2,1,0:T(8,128)(2,1)} %bitcast.53), calls=%async_computation.1 | async-start | bytes 4194304 | tf_op jit(solution)/shard_map/all_to_all | solution.py:69
  39.8 94.6 %all-gather.3.cloned.1.call-start = ((), (), s32[]{:S(2)}) async-start(), calls=%async_computation.5 | async-start | bytes 2621440 | tf_op jit(solution)/shard_map/all_gather | solution.py:87
  42.9 48.2 %copy-start.5 = (bf16[512,512]{1,0:T(8,128)(2,1)S(1)}, bf16[512,512]{1,0:T(8,128)(2,1)}, u32[]{:S(2)}) copy-start(bf16[512,512]{1,0:T(8,128)(2,1)} %param.23) | copy-start | bytes 1572868
  91.1 4.8 %copy-start.16 = (f32[512]{0:T(512)S(1)}, f32[512]{0:T(512)}, u32[]{:S(2)}) copy-start(f32[512]{0:T(512)} %param.25) | copy-start | bytes 6148
  95.9 6.0 %copy-start.1 = (bf16[512,1024]{1,0:T(8,128)(2,1)S(1)}, bf16[512,1024]{1,0:T(8,128)(2,1)}, u32[]{:S(2)}) copy-start(bf16[512,1024]{1,0:T(8,128)(2,1)} %param.26) | copy-start | bytes 3145732
  101.9 1.6 copy-start.2
  103.5 1.3 copy-start.8
  103.5 1.5 copy-start.4
  103.5 1.5 copy-start.13
  105.0 32.4 %copy-start.14 = (f32[1024]{0:T(1024)S(1)}, f32[1024]{0:T(1024)}, u32[]{:S(2)}) copy-start(f32[1024]{0:T(1024)} %param.27) | copy-start | bytes 12292
  105.0 32.4 %copy-start.15 = (f32[3,256]{1,0:T(4,128)S(1)}, f32[3,256]{1,0:T(4,128)}, u32[]{:S(2)}) copy-start(f32[3,256]{1,0:T(4,128)} %param.30) | copy-start | bytes 9220
  139.8 46.1 %copy-start.6 = (bf16[256,256]{1,0:T(8,128)(2,1)}, bf16[256,256]{1,0:T(8,128)(2,1)S(1)}, u32[]{:S(2)}) copy-start(bf16[256,256]{1,0:T(8,128)(2,1)S(1)} %fusion.50) | copy-start | bytes 393220
  139.8 12.2 %copy-start.9 = (s32[256,10]{0,1:T(8,128)S(1)}, s32[256,10]{0,1:T(8,128)}, u32[]{:S(2)}) copy-start(s32[256,10]{0,1:T(8,128)} %param.33) | copy-start | bytes 30724
  141.4 39.3 %all-to-all-start.2 = ((bf16[64,32,256]{2,1,0:T(8,128)(2,1)}), bf16[64,32,256]{2,1,0:T(8,128)(2,1)S(1)}, u32[]{:S(2)}, u32[]{:S(2)}) async-start(bf16[64,32,256]{2,1,0:T(8,128)(2,1)} %bitcast.55), calls=%async_computation.2 | async-start | bytes 2097152 | tf_op jit(solution)/shard_map/all_to_all | solution.py:106
  151.9 56.0 %reduce-scatter.2.cloned.1.call-start = ((), (), s32[]{:S(2)}) async-start(), calls=%async_computation.4 | async-start | bytes 655360 | tf_op jit(solution)/shard_map/reduce_scatter | solution.py:117
  180.7 5.2 %copy-start.7 = (bf16[256,1024]{1,0:T(8,128)(2,1)S(1)}, bf16[256,1024]{1,0:T(8,128)(2,1)}, u32[]{:S(2)}) copy-start(bf16[256,1024]{1,0:T(8,128)(2,1)} %param.36) | copy-start | bytes 1572868
  180.7 5.2 %copy-start.11 = (s32[256]{0:T(256)S(1)}, s32[256]{0:T(256)}, u32[]{:S(2)}) copy-start(s32[256]{0:T(256)} %param.34) | copy-start | bytes 3076
  185.9 22.0 %copy-start.10 = (f32[1024]{0:T(1024)S(1)}, f32[1024]{0:T(1024)}, u32[]{:S(2)}) copy-start(f32[1024]{0:T(1024)} %param.37) | copy-start | bytes 12292
Sparse Core Ops, SparseCore 0:
  104.9 29.4 all-gather.2
  188.6 19.3 reduce-scatter.1
